TPU v7x, 32 devices: a whole 2x2x4 slice. The times are simulated.
32 devices in a mesh: clips: 2 (over x), rows: 16 (over z, y, core).
Axes of the slice: x: 2, y: 2, z: 4, core: 2. Of those that a mesh axis runs over, the one named last changes fastest.
Arguments:
- frames: bfloat16 [2, 32, 128, 384], P('clips', 'rows'), parts along dimension 0, may hold values from -48 to 48
- norm_attn: float32 [384], replicated, may hold values from 0.25 to 1.75
- w_query: bfloat16 [384, 384], replicated, may hold values from -12 to 12
- w_key: bfloat16 [384, 384], replicated, may hold values from -12 to 12
- w_value: bfloat16 [384, 384], replicated, may hold values from -2 to 2
- w_out: bfloat16 [384, 384], replicated, may hold values from -9 to 9
- cache_one: bfloat16 [4, 32, 128, 384], P('clips', 'rows'), parts along dimension 0, may hold values from -6 to 6
- norm_conv: float32 [384], replicated, may hold values from 0.25 to 1.75
- conv_weight: bfloat16 [3, 3, 3, 384, 384], replicated, may hold values from -0.109375 to 0.109375
- w_up: bfloat16 [3, 3, 384, 192], replicated, may hold values from -0.109375 to 0.109375
Outputs:
- upsampled: bfloat16 [2, 64, 49152], P('clips', 'rows'), parts along dimension 0
There are 2 independent parts, one for each index of `clips`. A program takes and returns all parts, laid end to end along the dimension named above; an argument that names none is the same for every part. Nothing has to cross between parts.
All inputs are finite; a program needn't handle non-finite values.
Results may differ from a plain program's by a relative error of at most 0.013.
Values may be sent and summed in bfloat16 or wider, within the bound.
No kernel may reach another device: no remote copies, remote signals or barrier semaphores. Data moves between devices by JAX's collectives and lax.ppermute only.
A program may use at most 128 MiB of HBM per device.

v0:
```python
import jax
import jax.numpy as jnp
from jax import lax
from jax.sharding import PartitionSpec as P

EPS = 1e-06


def padded_2(array, sides, width):
    for axis, dim in sides:
        size, length = (lax.axis_size(axis), array.shape[dim])
        up = [(i, (i + 1) % size) for i in range(size - 1)]
        down = [(j, i) for i, j in up]
        last = lax.slice_in_dim(array, length - width, length, axis=dim)
        first = lax.slice_in_dim(array, 0, width, axis=dim)
        before = lax.ppermute(last, axis, up)
        after = lax.ppermute(first, axis, down)
        array = jnp.concatenate([before, array, after], axis=dim)
    return array


def rms_gain(values, gain):
    return values * lax.rsqrt(jnp.mean(values * values, axis=-1, keepdims=True) + EPS) * gain


def project(inputs, weight):
    return jnp.einsum("fqc,cd->fqd", inputs, weight, preferred_element_type=jnp.float32).astype(
        jnp.bfloat16
    )


def conv_core(padded, weight, frames_out, rows_out, cols_out):
    chans = padded.shape[-1]
    outs = weight.shape[-1]
    wide = jnp.concatenate(
        [padded[:, :, shift : shift + cols_out, :] for shift in range(3)], axis=-1
    )
    total = jnp.zeros((frames_out * rows_out * cols_out, outs), jnp.float32)
    for tstep in range(weight.shape[0]):
        for rstep in range(3):
            part = wide[tstep : tstep + frames_out, rstep : rstep + rows_out].reshape(-1, 3 * chans)
            total = total + jnp.dot(
                part,
                weight[tstep, rstep].reshape(3 * chans, outs),
                preferred_element_type=jnp.float32,
            )
    return total


def attend_block(carry, queries, keys, values, scale):
    running, denom, accum = carry
    scores = jnp.einsum("fqc,fkc->fqk", queries, keys, preferred_element_type=jnp.float32) * scale
    newtop = jnp.maximum(running, jnp.max(scores, axis=-1))
    expo = jnp.exp(scores - newtop[..., None])
    denom = jnp.sum(expo, axis=-1)
    accum = jnp.einsum(
        "fqk,fkc->fqc", expo.astype(jnp.bfloat16), values, preferred_element_type=jnp.float32
    )
    return (newtop, denom, accum)


def body(
    frames, norm_attn, w_query, w_key, w_value, w_out, cache_one, norm_conv, conv_weight, w_up
):
    nframes, nrows, ncols, chans = frames.shape
    scale = chans ** (-0.5)
    flat = frames.reshape(nframes, nrows * ncols, chans)
    normed = rms_gain(flat.astype(jnp.float32), norm_attn).astype(jnp.bfloat16)
    queries = project(normed, w_query)
    start_carry = (
        jnp.full((nframes, nrows * ncols), -1e30, jnp.float32),
        jnp.zeros((nframes, nrows * ncols), jnp.float32),
        jnp.zeros((nframes, nrows * ncols, chans), jnp.float32),
    )
    keys = project(normed, w_key).reshape(nframes, nrows, ncols, chans)
    values = project(normed, w_value).reshape(nframes, nrows, ncols, chans)
    keys_in = lax.all_gather(keys, "rows", axis=1, tiled=True).reshape(nframes, -1, chans)
    values_in = lax.all_gather(values, "rows", axis=1, tiled=True).reshape(nframes, -1, chans)
    carry = attend_block(start_carry, queries, keys_in, values_in, scale)
    attended = (carry[2] / carry[1][..., None]).astype(jnp.bfloat16)
    mixed = (
        flat.astype(jnp.float32)
        + jnp.einsum("fqc,cd->fqd", attended, w_out, preferred_element_type=jnp.float32)
    ).astype(jnp.bfloat16)
    activ = (
        jax.nn.silu(rms_gain(mixed.astype(jnp.float32), norm_conv))
        .astype(jnp.bfloat16)
        .reshape(nframes, nrows, ncols, chans)
    )
    stack = jnp.concatenate([cache_one, activ], axis=0)
    haloed = padded_2(stack, (("rows", 1),), 1)
    padded = jnp.pad(haloed, ((0, 0), (0, 0), (1, 1), (0, 0)))
    conv_out = (
        conv_core(padded, conv_weight, nframes, nrows, ncols)
        .astype(jnp.bfloat16)
        .reshape(nframes, nrows, ncols, chans)
    )
    extended = padded_2(conv_out, (("rows", 1),), 1)
    doubled = jnp.repeat(jnp.repeat(extended, 2, axis=1), 2, axis=2)[:, 1 : 2 * nrows + 3]
    padded_up = jnp.pad(doubled, ((0, 0), (0, 0), (1, 1), (0, 0)))
    result = conv_core(padded_up, w_up[None], nframes, 2 * nrows, 2 * ncols)
    return result.astype(jnp.bfloat16).reshape(nframes, 2 * nrows, 2 * ncols * w_up.shape[-1])


def solution(mesh):
    placed = (
        P("clips", "rows", None, None),
        P(),
        P(),
        P(),
        P(),
        P(),
        P("clips", "rows", None, None),
        P(),
        P(),
        P(),
    )
    return jax.shard_map(
        body, mesh=mesh, in_specs=placed, out_specs=P("clips", "rows", None), check_vma=False
    )
```

profile of v0, /device:TPU:5, one launch (start us, length us, event | category | flops | bytes accessed | tf_op | source)
XLA Modules:
  0.0 151.7 jit_solution(1694360441257205537)
XLA Ops:
  6.5 1.1 multiply_reduce_fusion.1
  7.6 1.0 fusion.29
  8.7 1.9 %convolution_convert_fusion.1 = bf16[256,384]{1,0:T(8,128)(2,1)} fusion(bf16[256,384]{1,0:T(8,128)(2,1)S(1)} %fusion.29, bf16[384,384]{1,0:T(8,128)(2,1)} %param.13), kind=kOutput, calls=%fused_computation.30 | convolution fusion | flops 75595776 | bytes 688128 | tf_op jit(solution)/shard_map/fqc,cd->fqd/dot_general | solution.py:27
  10.7 1.9 %convolution_convert_fusion = bf16[256,384]{1,0:T(8,128)(2,1)} fusion(bf16[256,384]{1,0:T(8,128)(2,1)S(1)} %fusion.29, bf16[384,384]{1,0:T(8,128)(2,1)} %param.14), kind=kOutput, calls=%fused_computation.29 | convolution fusion | flops 75595776 | bytes 688128 | tf_op jit(solution)/shard_map/fqc,cd->fqd/dot_general | solution.py:27
  12.6 44.3 %all-gather.3.cloned.1.call-done = bf16[1,32,128,384]{3,2,0,1:T(8,128)(2,1)} async-done(((bf16[1,2,128,384]{3,2,0,1:T(8,128)(2,1)}), bf16[1,32,128,384]{3,2,0,1:T(8,128)(2,1)}) %all-gather.3.cloned.1.call-update) | async-done | bytes 3145744 | tf_op jit(solution)/shard_map/all_gather | solution.py:77
  56.9 5.3 %fusion.38 = (f32[256]{0:T(256)S(1)}, f32[256,4096]{1,0:T(8,128)}) fusion(bf16[4096,384]{1,0:T(8,128)(2,1)} %bitcast.108, bf16[256,384]{1,0:T(8,128)(2,1)S(1)} %fusion.29, bf16[384,384]{1,0:T(8,128)(2,1)S(1)} %copy-done), kind=kOutput, calls=%fused_computation.59 | convolution fusion | flops 882999040 | bytes 7832576 | tf_op jit(solution)/shard_map/fqc,fkc->fqk/dot_general | solution.py:52
  62.3 3.0 %fusion = f32[256]{0:T(256)S(1)} fusion(f32[256,4096]{1,0:T(8,128)} %get-tuple-element.38, f32[256]{0:T(256)S(1)} %broadcast_maximum_fusion), kind=kLoop, calls=%fused_computation.4 | loop fusion | flops 2096896 | bytes 4196352 | tf_op jit(solution)/shard_map/reduce_sum | solution.py:55
  65.2 37.8 %all-gather.5.cloned.1.call-done = bf16[1,32,128,384]{3,2,0,1:T(8,128)(2,1)} async-done(((bf16[1,2,128,384]{3,2,0,1:T(8,128)(2,1)}), bf16[1,32,128,384]{3,2,0,1:T(8,128)(2,1)}) %all-gather.5.cloned.1.call-update) | async-done | bytes 3145744 | tf_op jit(solution)/shard_map/all_gather | solution.py:78
  103.0 4.8 %multiply_reduce_fusion = (f32[256]{0:T(256)S(1)}, f32[256,384]{1,0:T(8,128)S(1)}) fusion(bf16[384,384]{1,0:T(8,128)(2,1)S(1)} %copy-done.9, bf16[4096,384]{1,0:T(8,128)(2,1)} %bitcast.130, f32[256,4096]{1,0:T(8,128)} %get-tuple-element.38, f32[256]{0:T(256)S(1)} %broadcast_maximum_fusion, f32[256]{0:T(256)S(1)} %fusion, bf16[256,384]{1,0:T(8,128)(2,1)S(1)} %bitcast.127), kind=kOutput, calls=%fused_computation.45 | convolution fusion | flops 883687168 | bytes 8227840 | tf_op jit(solution)/shard_map/fqc,cd->fqd/dot_general | solution.py:83
  108.2 4.1 %collective-permute-start = (bf16[3,1,128,384]{3,2,1,0:T(8,128)(2,1)S(1)}, bf16[3,1,128,384]{3,2,1,0:T(8,128)(2,1)S(1)}, u32[]{:S(2)}, u32[]{:S(2)}) collective-permute-start(bf16[3,1,128,384]{3,2,1,0:T(8,128)(2,1)S(1)} %get-tuple-element.33), channel_id=1, source_target_pairs={{0,1},{1,2},{2,3},{3,4},{4,5},{5,6},{6,7},{7,8},{8,9},{9,10},{10,1... | collective-permute-start | bytes 884744 | tf_op jit(solution)/shard_map/ppermute | solution.py:16
  112.3 1.9 %collective-permute-start.1 = (bf16[3,1,128,384]{3,2,1,0:T(8,128)(2,1)S(1)}, bf16[3,1,128,384]{3,2,1,0:T(8,128)(2,1)S(1)}, u32[]{:S(2)}, u32[]{:S(2)}) collective-permute-start(bf16[3,1,128,384]{3,2,1,0:T(8,128)(2,1)S(1)} %get-tuple-element.34), channel_id=1, source_target_pairs={{1,0},{2,1},{3,2},{4,3},{5,4},{6,5},{7,6},{8,7},{9,8},{10,9},{11,1... | collective-permute-start | bytes 884744 | tf_op jit(solution)/shard_map/ppermute | solution.py:17
  114.2 3.9 %fusion.32 = (bf16[1,1,3,384,384]{4,3,2,1,0:T(8,128)(2,1)S(1)}, bf16[1,1,3,384,384]{4,3,2,1,0:T(8,128)(2,1)S(1)}, bf16[1,1,3,384,384]{4,3,2,1,0:T(8,128)(2,1)S(1...) fusion(bf16[3,3,3,384,384]{4,3,2,1,0:T(8,128)(2,1)} %param.18), kind=kLoop, calls=%fused_computation.53 | loop fusion | bytes 15925248 | tf_op jit(solution)/shard_map/slice | solution.py:44
  118.2 3.1 %collective-permute-done.1 = bf16[3,1,128,384]{3,2,1,0:T(8,128)(2,1)S(1)} collective-permute-done((bf16[3,1,128,384]{3,2,1,0:T(8,128)(2,1)S(1)}, bf16[3,1,128,384]{3,2,1,0:T(8,128)(2,1)S(1)}, u32[]{:S(2)}, u32[]{:S(2)}) %collective-permute-start.1) | collective-permute-done | bytes 294944 | tf_op jit(solution)/shard_map/ppermute | solution.py:17
  127.9 1.9 %collective-permute-start.2 = (bf16[1,1,128,384]{3,2,1,0:T(8,128)(2,1)S(1)}, bf16[1,1,128,384]{3,2,1,0:T(8,128)(2,1)S(1)}, u32[]{:S(2)}, u32[]{:S(2)}) collective-permute-start(bf16[1,1,128,384]{3,2,1,0:T(8,128)(2,1)S(1)} %get-tuple-element.35), channel_id=1, source_target_pairs={{0,1},{1,2},{2,3},{3,4},{4,5},{5,6},{6,7},{7,8},{8,9},{9,10},{10,1... | collective-permute-start | bytes 294920 | tf_op jit(solution)/shard_map/ppermute | solution.py:16
  129.9 2.6 %collective-permute-start.3 = (bf16[1,1,128,384]{3,2,1,0:T(8,128)(2,1)S(1)}, bf16[1,1,128,384]{3,2,1,0:T(8,128)(2,1)S(1)}, u32[]{:S(2)}, u32[]{:S(2)}) collective-permute-start(bf16[1,1,128,384]{3,2,1,0:T(8,128)(2,1)S(1)} %get-tuple-element.36), channel_id=1, source_target_pairs={{1,0},{2,1},{3,2},{4,3},{5,4},{6,5},{7,6},{8,7},{9,8},{10,9},{11,1... | collective-permute-start | bytes 294920 | tf_op jit(solution)/shard_map/ppermute | solution.py:17
  133.0 0.8 copy.21
  134.2 0.8 copy.22
  135.4 0.8 copy.23
  136.8 0.8 broadcast_in_dim.25
  139.3 0.9 fusion.33
  140.3 0.9 fusion.49
  141.4 0.9 convolution_add_fusion.1
  142.4 0.9 fusion.9
  143.5 1.3 reshape.221
  (57 shorter events, 10.9 us)
Async XLA Ops:
  6.5 50.4 %copy-start = (bf16[384,384]{1,0:T(8,128)(2,1)S(1)}, bf16[384,384]{1,0:T(8,128)(2,1)}, u32[]{:S(2)}) copy-start(bf16[384,384]{1,0:T(8,128)(2,1)} %param.12) | copy-start | bytes 884740
  6.5 50.4 %all-gather.3.cloned.1.call-start = ((), (), s32[]{:S(2)}) async-start(), calls=%async_computation | async-start | bytes 3342336 | tf_op jit(solution)/shard_map/all_gather | solution.py:77
  10.6 92.4 %all-gather.5.cloned.1.call-start = ((), (), s32[]{:S(2)}) async-start(), calls=%async_computation.1 | async-start | bytes 3342336 | tf_op jit(solution)/shard_map/all_gather | solution.py:78
  62.2 40.8 %copy-start.7 = (bf16[1,2,128,384]{3,2,1,0:T(8,128)(2,1)S(1)}, bf16[1,2,128,384]{3,2,1,0:T(8,128)(2,1)}, u32[]{:S(2)}) copy-start(bf16[1,2,128,384]{3,2,1,0:T(8,128)(2,1)} %param.10) | copy-start | bytes 589828
  62.2 40.8 %copy-start.9 = (bf16[384,384]{1,0:T(8,128)(2,1)S(1)}, bf16[384,384]{1,0:T(8,128)(2,1)}, u32[]{:S(2)}) copy-start(bf16[384,384]{1,0:T(8,128)(2,1)} %param.15) | copy-start | bytes 884740
  103.0 4.8 %copy-start.8 = (f32[384]{0:T(512)S(1)}, f32[384]{0:T(512)}, u32[]{:S(2)}) copy-start(f32[384]{0:T(512)} %param.17) | copy-start | bytes 4612
  103.0 5.0 %copy-start.2 = (bf16[2,2,128,384]{3,2,1,0:T(8,128)(2,1)S(1)}, bf16[2,2,128,384]{3,2,1,0:T(8,128)(2,1)}, u32[]{:S(2)}) copy-start(bf16[2,2,128,384]{3,2,1,0:T(8,128)(2,1)} %param.16) | copy-start | bytes 1179652
  108.2 10.0 %collective-permute-start = (bf16[3,1,128,384]{3,2,1,0:T(8,128)(2,1)S(1)}, bf16[3,1,128,384]{3,2,1,0:T(8,128)(2,1)S(1)}, u32[]{:S(2)}, u32[]{:S(2)}) collective-permute-start(bf16[3,1,128,384]{3,2,1,0:T(8,128)(2,1)S(1)} %get-tuple-element.33), channel_id=1, source_target_pairs={{0,1},{1,2},{2,3},{3,4},{4,5},{5,6},{6,7},{7,8},{8,9},{9,10},{10,1... | collective-permute-start | bytes 884744 | tf_op jit(solution)/shard_map/ppermute | solution.py:16
  112.3 8.9 %collective-permute-start.1 = (bf16[3,1,128,384]{3,2,1,0:T(8,128)(2,1)S(1)}, bf16[3,1,128,384]{3,2,1,0:T(8,128)(2,1)S(1)}, u32[]{:S(2)}, u32[]{:S(2)}) collective-permute-start(bf16[3,1,128,384]{3,2,1,0:T(8,128)(2,1)S(1)} %get-tuple-element.34), channel_id=1, source_target_pairs={{1,0},{2,1},{3,2},{4,3},{5,4},{6,5},{7,6},{8,7},{9,8},{10,9},{11,1... | collective-permute-start | bytes 884744 | tf_op jit(solution)/shard_map/ppermute | solution.py:17
  127.2 5.2 %copy-start.6 = (bf16[3,3,384,192]{2,3,1,0:T(8,128)(2,1)S(1)}, bf16[3,3,384,192]{2,3,1,0:T(8,128)(2,1)}, u32[]{:S(2)}) copy-start(bf16[3,3,384,192]{2,3,1,0:T(8,128)(2,1)} %param.19) | copy-start | bytes 3981316
  127.9 8.3 %collective-permute-start.2 = (bf16[1,1,128,384]{3,2,1,0:T(8,128)(2,1)S(1)}, bf16[1,1,128,384]{3,2,1,0:T(8,128)(2,1)S(1)}, u32[]{:S(2)}, u32[]{:S(2)}) collective-permute-start(bf16[1,1,128,384]{3,2,1,0:T(8,128)(2,1)S(1)} %get-tuple-element.35), channel_id=1, source_target_pairs={{0,1},{1,2},{2,3},{3,4},{4,5},{5,6},{6,7},{7,8},{8,9},{9,10},{10,1... | collective-permute-start | bytes 294920 | tf_op jit(solution)/shard_map/ppermute | solution.py:16
  129.9 6.8 %collective-permute-start.3 = (bf16[1,1,128,384]{3,2,1,0:T(8,128)(2,1)S(1)}, bf16[1,1,128,384]{3,2,1,0:T(8,128)(2,1)S(1)}, u32[]{:S(2)}, u32[]{:S(2)}) collective-permute-start(bf16[1,1,128,384]{3,2,1,0:T(8,128)(2,1)S(1)} %get-tuple-element.36), channel_id=1, source_target_pairs={{1,0},{2,1},{3,2},{4,3},{5,4},{6,5},{7,6},{8,7},{9,8},{10,9},{11,1... | collective-permute-start | bytes 294920 | tf_op jit(solution)/shard_map/ppermute | solution.py:17
  139.3 1.0 copy-start.4
  140.3 1.0 copy-start.3
  141.4 1.0 copy-start.5
  142.4 2.5 %copy-start.1 = (bf16[384,384]{1,0:T(8,128)(2,1)S(1)}, bf16[384,384]{1,0:T(8,128)(2,1)}, u32[]{:S(2)}) copy-start(bf16[384,384]{1,0:T(8,128)(2,1)} %param.12) | copy-start | bytes 884740
Sparse Core Ops, SparseCore 0:
  10.8 46.1 all-gather.2
  59.2 43.7 all-gather.4
where the time goes:
time: 152 us
  waiting for transfers between devices  85.7 us (56%)
  matrix products  21.2 us (14%)
  local copies, waits for them, and re-layouts  13.9 us (9%)
  between operations  13.7 us (9%)
  starting transfers between devices  10.6 us (7%)
  other arithmetic  6.63 us (4%)
    all_gather x1, waiting for transfers between devices, body(): lax.all_gather(keys, 'rows', axis=1, tiled=True).reshape(nframes, -1, chans)  44.3 us
    all_gather x1, waiting for transfers between devices, body(): lax.all_gather(values, 'rows', axis=1, tiled=True)  37.8 us
    dot_general x12, matrix products, conv_core(): jnp.dot(part, weight[tstep, rstep].reshape(3 * chans, outs), preferred_el...  7.22 us
    ppermute x2, starting transfers between devices, padded_2(): before = lax.ppermute(last, axis, up)  6.06 us
    dot_general x1, matrix products, attend_block(): jnp.einsum('fqc,fkc->fqk', queries, keys, preferred_element_type=jnp.floa...  5.32 us
    slice x5, local copies, waits for them, and re-layouts, conv_core(): weight[tstep, rstep].reshape(3 * chans, outs)  5.2 us
    dot_general x1, matrix products, body(): jnp.einsum('fqc,cd->fqd', attended, w_out, preferred_element_type=jnp.flo...  4.82 us
    ppermute x2, starting transfers between devices, padded_2(): after = lax.ppermute(first, axis, down)  4.51 us
  transfers between devices with their start and end apart: 6, of which 4 were waited for; matrix products, arithmetic and copies ran while one was open for 12% of the time, Pallas kernels for 0%

commit v1 on v0

--- a/solution.py
+++ b/solution.py
@@ -4,6 +4,27 @@
 from jax.sharding import PartitionSpec as P
 
 EPS = 1e-06
+
+
+def collect(x, axis, dim):
+    peers, index, span = (lax.axis_size(axis), lax.axis_index(axis), x.shape[dim])
+    upward = [(i, (i + 1) % peers) for i in range(peers)]
+    downward = [(i, (i - 1) % peers) for i in range(peers)]
+    whole = jnp.zeros((*x.shape[:dim], peers * span, *x.shape[dim + 1 :]), x.dtype)
+    whole = lax.dynamic_update_slice_in_dim(whole, x, index * span, axis=dim)
+    from_left = from_right = x
+    half = peers // 2
+    for step in range(1, half + 1):
+        from_left = lax.ppermute(from_left, axis, upward)
+        whole = lax.dynamic_update_slice_in_dim(
+            whole, from_left, (index - step) % peers * span, axis=dim
+        )
+        if step < peers - half:
+            from_right = lax.ppermute(from_right, axis, downward)
+            whole = lax.dynamic_update_slice_in_dim(
+                whole, from_right, (index + step) % peers * span, axis=dim
+            )
+    return whole
 
 
 def padded_2(array, sides, width):
@@ -75,7 +96,7 @@
     keys = project(normed, w_key).reshape(nframes, nrows, ncols, chans)
     values = project(normed, w_value).reshape(nframes, nrows, ncols, chans)
     keys_in = lax.all_gather(keys, "rows", axis=1, tiled=True).reshape(nframes, -1, chans)
-    values_in = lax.all_gather(values, "rows", axis=1, tiled=True).reshape(nframes, -1, chans)
+    values_in = collect(values, "rows", 1).reshape(nframes, -1, chans)
     carry = attend_block(start_carry, queries, keys_in, values_in, scale)
     attended = (carry[2] / carry[1][..., None]).astype(jnp.bfloat16)
     mixed = (

time: 152 us -> 138 us (0.908)
  the two profiles are of different devices: /device:TPU:5 before, /device:TPU:1 now
where the time goes in v1:
time: 138 us
  starting transfers between devices  57.8 us (42%)
  matrix products  22.4 us (16%)
  waiting for transfers between devices  19.6 us (14%)
  local copies, waits for them, and re-layouts  17.6 us (13%)
  between operations  13.9 us (10%)
  other arithmetic  6.62 us (5%)
    ppermute x7, starting transfers between devices, collect(): from_right = lax.ppermute(from_right, axis, downward)  35.1 us
    ppermute x8, waiting for transfers between devices, collect(): from_left = lax.ppermute(from_left, axis, upward)  14.1 us
    ppermute x2, starting transfers between devices, padded_2(): after = lax.ppermute(first, axis, down)  11 us
    ppermute x8, starting transfers between devices, collect(): from_left = lax.ppermute(from_left, axis, upward)  7.85 us
    dot_general x12, matrix products, conv_core(): jnp.dot(part, weight[tstep, rstep].reshape(3 * chans, outs), preferred_el...  7.17 us
    dot_general x1, matrix products, attend_block(): jnp.einsum('fqc,fkc->fqk', queries, keys, preferred_element_type=jnp.floa...  6.52 us
    ppermute x7, waiting for transfers between devices, collect(): from_right = lax.ppermute(from_right, axis, downward)  5.49 us
    slice x5, local copies, waits for them, and re-layouts, conv_core(): weight[tstep, rstep].reshape(3 * chans, outs)  5.2 us
  transfers between devices with their start and end apart: 20, of which 13 were waited for; matrix products, arithmetic and copies ran while one was open for 10% of the time, Pallas kernels for 0%

profile of v1, /device:TPU:1, one launch (start us, length us, event | category | flops | bytes accessed | tf_op | source)
XLA Modules:
  0.0 137.9 jit_solution(13766560684372826078)
XLA Ops:
  6.5 1.1 multiply_reduce_fusion.1
  8.7 2.0 %convolution_convert_fusion.1 = bf16[256,384]{1,0:T(8,128)(2,1)} fusion(bf16[256,384]{1,0:T(8,128)(2,1)S(1)} %fusion.29, bf16[384,384]{1,0:T(8,128)(2,1)} %param.13), kind=kOutput, calls=%fused_computation.30 | convolution fusion | flops 75595776 | bytes 688128 | tf_op jit(solution)/shard_map/fqc,cd->fqd/dot_general | solution.py:48
  10.7 1.9 %convolution_convert_fusion = bf16[256,384]{1,0:T(8,128)(2,1)} fusion(bf16[256,384]{1,0:T(8,128)(2,1)S(1)} %fusion.29, bf16[384,384]{1,0:T(8,128)(2,1)} %param.14), kind=kOutput, calls=%fused_computation.29 | convolution fusion | flops 75595776 | bytes 688128 | tf_op jit(solution)/shard_map/fqc,cd->fqd/dot_general | solution.py:48
  12.6 2.6 %collective-permute-start = (bf16[1,2,128,384]{3,2,1,0:T(8,128)(2,1)}, bf16[1,2,128,384]{3,2,1,0:T(8,128)(2,1)}, u32[]{:S(2)}, u32[]{:S(2)}) collective-permute-start(bf16[1,2,128,384]{3,2,1,0:T(8,128)(2,1)} %bitcast.5), channel_id=1, source_target_pairs={{0,1},{1,2},{2,3},{3,4},{4,5},{5,6},{6,7},{7,8},{8,9},{9,10},{10,1... | collective-permute-start | bytes 589832 | tf_op jit(solution)/shard_map/ppermute | solution.py:18
  16.7 1.5 %collective-permute-done = bf16[1,2,128,384]{3,2,1,0:T(8,128)(2,1)} collective-permute-done((bf16[1,2,128,384]{3,2,1,0:T(8,128)(2,1)}, bf16[1,2,128,384]{3,2,1,0:T(8,128)(2,1)}, u32[]{:S(2)}, u32[]{:S(2)}) %collective-permute-start) | collective-permute-done | bytes 196640 | tf_op jit(solution)/shard_map/ppermute | solution.py:18
  18.2 2.5 %collective-permute-start.2 = (bf16[1,2,128,384]{3,2,1,0:T(8,128)(2,1)}, bf16[1,2,128,384]{3,2,1,0:T(8,128)(2,1)S(1)}, u32[]{:S(2)}, u32[]{:S(2)}) collective-permute-start(bf16[1,2,128,384]{3,2,1,0:T(8,128)(2,1)} %collective-permute-done), channel_id=1, source_target_pairs={{0,1},{1,2},{2,3},{3,4},{4,5},{5,6},{6,7},{7,8},{8,9},{9,10},{10,1... | collective-permute-start | bytes 589832 | tf_op jit(solution)/shard_map/ppermute | solution.py:18
  20.6 2.1 %collective-permute-done.1 = bf16[1,2,128,384]{3,2,1,0:T(8,128)(2,1)} collective-permute-done((bf16[1,2,128,384]{3,2,1,0:T(8,128)(2,1)}, bf16[1,2,128,384]{3,2,1,0:T(8,128)(2,1)}, u32[]{:S(2)}, u32[]{:S(2)}) %collective-permute-start.1) | collective-permute-done | bytes 196640 | tf_op jit(solution)/shard_map/ppermute | solution.py:23
  24.7 2.7 %collective-permute-done.2 = bf16[1,2,128,384]{3,2,1,0:T(8,128)(2,1)S(1)} collective-permute-done((bf16[1,2,128,384]{3,2,1,0:T(8,128)(2,1)}, bf16[1,2,128,384]{3,2,1,0:T(8,128)(2,1)S(1)}, u32[]{:S(2)}, u32[]{:S(2)}) %collective-permute-start.2) | collective-permute-done | bytes 196640 | tf_op jit(solution)/shard_map/ppermute | solution.py:18
  27.4 2.5 %collective-permute-start.4 = (bf16[1,2,128,384]{3,2,1,0:T(8,128)(2,1)S(1)}, bf16[1,2,128,384]{3,2,1,0:T(8,128)(2,1)S(1)}, u32[]{:S(2)}, u32[]{:S(2)}) collective-permute-start(bf16[1,2,128,384]{3,2,1,0:T(8,128)(2,1)S(1)} %collective-permute-done.2), channel_id=1, source_target_pairs={{0,1},{1,2},{2,3},{3,4},{4,5},{5,6},{6,7},{7,8},{8,9},{9,10},{10,1... | collective-permute-start | bytes 589832 | tf_op jit(solution)/shard_map/ppermute | solution.py:18
  29.9 4.0 %collective-permute-start.5 = (bf16[1,2,128,384]{3,2,1,0:T(8,128)(2,1)S(1)}, bf16[1,2,128,384]{3,2,1,0:T(8,128)(2,1)S(1)}, u32[]{:S(2)}, u32[]{:S(2)}) collective-permute-start(bf16[1,2,128,384]{3,2,1,0:T(8,128)(2,1)S(1)} %collective-permute-done.3), channel_id=1, source_target_pairs={{0,15},{1,0},{2,1},{3,2},{4,3},{5,4},{6,5},{7,6},{8,7},{9,8},{10,9... | collective-permute-start | bytes 589832 | tf_op jit(solution)/shard_map/ppermute | solution.py:23
  35.5 7.8 %collective-permute-start.7 = (bf16[1,2,128,384]{3,2,1,0:T(8,128)(2,1)S(1)}, bf16[1,2,128,384]{3,2,1,0:T(8,128)(2,1)S(1)}, u32[]{:S(2)}, u32[]{:S(2)}) collective-permute-start(bf16[1,2,128,384]{3,2,1,0:T(8,128)(2,1)S(1)} %collective-permute-done.5), channel_id=1, source_target_pairs={{0,15},{1,0},{2,1},{3,2},{4,3},{5,4},{6,5},{7,6},{8,7},{9,8},{10,9... | collective-permute-start | bytes 589832 | tf_op jit(solution)/shard_map/ppermute | solution.py:23
  44.4 9.3 %collective-permute-start.9 = (bf16[1,2,128,384]{3,2,1,0:T(8,128)(2,1)S(1)}, bf16[1,2,128,384]{3,2,1,0:T(8,128)(2,1)S(1)}, u32[]{:S(2)}, u32[]{:S(2)}) collective-permute-start(bf16[1,2,128,384]{3,2,1,0:T(8,128)(2,1)S(1)} %collective-permute-done.7), channel_id=1, source_target_pairs={{0,15},{1,0},{2,1},{3,2},{4,3},{5,4},{6,5},{7,6},{8,7},{9,8},{10,9... | collective-permute-start | bytes 589832 | tf_op jit(solution)/shard_map/ppermute | solution.py:23
  55.7 7.1 %collective-permute-start.11 = (bf16[1,2,128,384]{3,2,1,0:T(8,128)(2,1)S(1)}, bf16[1,2,128,384]{3,2,1,0:T(8,128)(2,1)S(1)}, u32[]{:S(2)}, u32[]{:S(2)}) collective-permute-start(bf16[1,2,128,384]{3,2,1,0:T(8,128)(2,1)S(1)} %collective-permute-done.9), channel_id=1, source_target_pairs={{0,15},{1,0},{2,1},{3,2},{4,3},{5,4},{6,5},{7,6},{8,7},{9,8},{10,9... | collective-permute-start | bytes 589832 | tf_op jit(solution)/shard_map/ppermute | solution.py:23
  63.8 6.8 %collective-permute-start.13 = (bf16[1,2,128,384]{3,2,1,0:T(8,128)(2,1)S(1)}, bf16[1,2,128,384]{3,2,1,0:T(8,128)(2,1)S(1)}, u32[]{:S(2)}, u32[]{:S(2)}) collective-permute-start(bf16[1,2,128,384]{3,2,1,0:T(8,128)(2,1)S(1)} %collective-permute-done.11), channel_id=1, source_target_pairs={{0,15},{1,0},{2,1},{3,2},{4,3},{5,4},{6,5},{7,6},{8,7},{9,8},{10,9... | collective-permute-start | bytes 589832 | tf_op jit(solution)/shard_map/ppermute | solution.py:23
  71.7 7.2 %collective-permute-done.14 = bf16[1,2,128,384]{3,2,1,0:T(8,128)(2,1)S(1)} collective-permute-done((bf16[1,2,128,384]{3,2,1,0:T(8,128)(2,1)S(1)}, bf16[1,2,128,384]{3,2,1,0:T(8,128)(2,1)S(1)}, u32[]{:S(2)}, u32[]{:S(2)}) %collective-permute-start.14) | collective-permute-done | bytes 196640 | tf_op jit(solution)/shard_map/ppermute | solution.py:18
  79.1 6.5 %fusion.38 = (f32[256]{0:T(256)S(1)}, f32[256,4096]{1,0:T(8,128)}) fusion(bf16[4096,384]{1,0:T(8,128)(2,1)} %bitcast.107, bf16[256,384]{1,0:T(8,128)(2,1)} %copy-done.4, bf16[384,384]{1,0:T(8,128)(2,1)S(1)} %copy-done), kind=kOutput, calls=%fused_computation.75 | convolution fusion | flops 882999040 | bytes 7832576 | tf_op jit(solution)/shard_map/fqc,fkc->fqk/dot_general | solution.py:73
  85.6 2.9 %fusion = f32[256]{0:T(256)S(1)} fusion(f32[256,4096]{1,0:T(8,128)} %get-tuple-element.38, f32[256]{0:T(256)S(1)} %broadcast_maximum_fusion), kind=kLoop, calls=%fused_computation.4 | loop fusion | flops 2096896 | bytes 4196352 | tf_op jit(solution)/shard_map/reduce_sum | solution.py:76
  88.6 4.8 %multiply_reduce_fusion = (f32[256]{0:T(256)S(1)}, f32[256,384]{1,0:T(8,128)S(1)}) fusion(bf16[384,384]{1,0:T(8,128)(2,1)S(1)} %copy-done.11, bf16[4096,384]{1,0:T(8,128)(2,1)} %bitcast.105, f32[256,4096]{1,0:T(8,128)} %get-tuple-element.38, f32[256]{0:T(256)S(1)} %broadcast_maximum_fusion, f32[256]{0:T(256)S(1)} %fusion, bf16[256,384]{1,0:T(8,128)(2,1)S(1)} %bitcast.126), kind=kOutput, calls=%fused_computation.45 | convolution fusion | flops 883687168 | bytes 8227840 | tf_op jit(solution)/shard_map/fqc,cd->fqd/dot_general | solution.py:104
  93.7 1.9 %collective-permute-start.15 = (bf16[3,1,128,384]{3,2,1,0:T(8,128)(2,1)S(1)}, bf16[3,1,128,384]{3,2,1,0:T(8,128)(2,1)S(1)}, u32[]{:S(2)}, u32[]{:S(2)}) collective-permute-start(bf16[3,1,128,384]{3,2,1,0:T(8,128)(2,1)S(1)} %get-tuple-element.33), channel_id=1, source_target_pairs={{0,1},{1,2},{2,3},{3,4},{4,5},{5,6},{6,7},{7,8},{8,9},{9,10},{10,1... | collective-permute-start | bytes 884744 | tf_op jit(solution)/shard_map/ppermute | solution.py:37
  95.7 8.3 %collective-permute-start.16 = (bf16[3,1,128,384]{3,2,1,0:T(8,128)(2,1)S(1)}, bf16[3,1,128,384]{3,2,1,0:T(8,128)(2,1)S(1)}, u32[]{:S(2)}, u32[]{:S(2)}) collective-permute-start(bf16[3,1,128,384]{3,2,1,0:T(8,128)(2,1)S(1)} %get-tuple-element.34), channel_id=1, source_target_pairs={{1,0},{2,1},{3,2},{4,3},{5,4},{6,5},{7,6},{8,7},{9,8},{10,9},{11,1... | collective-permute-start | bytes 884744 | tf_op jit(solution)/shard_map/ppermute | solution.py:38
  104.0 3.9 %fusion.32 = (bf16[1,1,3,384,384]{4,3,2,1,0:T(8,128)(2,1)S(1)}, bf16[1,1,3,384,384]{4,3,2,1,0:T(8,128)(2,1)S(1)}, bf16[1,1,3,384,384]{4,3,2,1,0:T(8,128)(2,1)S(1...) fusion(bf16[3,3,3,384,384]{4,3,2,1,0:T(8,128)(2,1)} %param.18), kind=kLoop, calls=%fused_computation.69 | loop fusion | bytes 15925248 | tf_op jit(solution)/shard_map/slice | solution.py:65
  114.6 1.9 %collective-permute-start.17 = (bf16[1,1,128,384]{3,2,1,0:T(8,128)(2,1)S(1)}, bf16[1,1,128,384]{3,2,1,0:T(8,128)(2,1)S(1)}, u32[]{:S(2)}, u32[]{:S(2)}) collective-permute-start(bf16[1,1,128,384]{3,2,1,0:T(8,128)(2,1)S(1)} %get-tuple-element.35), channel_id=1, source_target_pairs={{0,1},{1,2},{2,3},{3,4},{4,5},{5,6},{6,7},{7,8},{8,9},{9,10},{10,1... | collective-permute-start | bytes 294920 | tf_op jit(solution)/shard_map/ppermute | solution.py:37
  116.5 2.6 %collective-permute-start.18 = (bf16[1,1,128,384]{3,2,1,0:T(8,128)(2,1)S(1)}, bf16[1,1,128,384]{3,2,1,0:T(8,128)(2,1)S(1)}, u32[]{:S(2)}, u32[]{:S(2)}) collective-permute-start(bf16[1,1,128,384]{3,2,1,0:T(8,128)(2,1)S(1)} %get-tuple-element.36), channel_id=1, source_target_pairs={{1,0},{2,1},{3,2},{4,3},{5,4},{6,5},{7,6},{8,7},{9,8},{10,9},{11,1... | collective-permute-start | bytes 294920 | tf_op jit(solution)/shard_map/ppermute | solution.py:38
  129.7 1.3 reshape.221
  (105 shorter events, 28.4 us)
Async XLA Ops:
  6.5 72.5 %copy-start = (bf16[384,384]{1,0:T(8,128)(2,1)S(1)}, bf16[384,384]{1,0:T(8,128)(2,1)}, u32[]{:S(2)}) copy-start(bf16[384,384]{1,0:T(8,128)(2,1)} %param.12) | copy-start | bytes 884740
  6.5 72.5 %all-gather.2.cloned.1.call-start = ((), (), s32[]{:S(2)}) async-start(), calls=%async_computation | async-start | bytes 3342336 | tf_op jit(solution)/shard_map/all_gather | solution.py:98
  8.7 6.5 %copy-start.4 = (bf16[256,384]{1,0:T(8,128)(2,1)}, bf16[256,384]{1,0:T(8,128)(2,1)S(1)}, u32[]{:S(2)}) copy-start(bf16[256,384]{1,0:T(8,128)(2,1)S(1)} %fusion.29) | copy-start | bytes 589828
  12.6 5.5 %collective-permute-start = (bf16[1,2,128,384]{3,2,1,0:T(8,128)(2,1)}, bf16[1,2,128,384]{3,2,1,0:T(8,128)(2,1)}, u32[]{:S(2)}, u32[]{:S(2)}) collective-permute-start(bf16[1,2,128,384]{3,2,1,0:T(8,128)(2,1)} %bitcast.5), channel_id=1, source_target_pairs={{0,1},{1,2},{2,3},{3,4},{4,5},{5,6},{6,7},{7,8},{8,9},{9,10},{10,1... | collective-permute-start | bytes 589832 | tf_op jit(solution)/shard_map/ppermute | solution.py:18
  15.2 7.5 %collective-permute-start.1 = (bf16[1,2,128,384]{3,2,1,0:T(8,128)(2,1)}, bf16[1,2,128,384]{3,2,1,0:T(8,128)(2,1)}, u32[]{:S(2)}, u32[]{:S(2)}) collective-permute-start(bf16[1,2,128,384]{3,2,1,0:T(8,128)(2,1)} %bitcast.5), channel_id=1, source_target_pairs={{0,15},{1,0},{2,1},{3,2},{4,3},{5,4},{6,5},{7,6},{8,7},{9,8},{10,9... | collective-permute-start | bytes 589832 | tf_op jit(solution)/shard_map/ppermute | solution.py:23
  18.2 9.2 %collective-permute-start.2 = (bf16[1,2,128,384]{3,2,1,0:T(8,128)(2,1)}, bf16[1,2,128,384]{3,2,1,0:T(8,128)(2,1)S(1)}, u32[]{:S(2)}, u32[]{:S(2)}) collective-permute-start(bf16[1,2,128,384]{3,2,1,0:T(8,128)(2,1)} %collective-permute-done), channel_id=1, source_target_pairs={{0,1},{1,2},{2,3},{3,4},{4,5},{5,6},{6,7},{7,8},{8,9},{9,10},{10,1... | collective-permute-start | bytes 589832 | tf_op jit(solution)/shard_map/ppermute | solution.py:18
  22.8 7.1 %collective-permute-start.3 = (bf16[1,2,128,384]{3,2,1,0:T(8,128)(2,1)}, bf16[1,2,128,384]{3,2,1,0:T(8,128)(2,1)S(1)}, u32[]{:S(2)}, u32[]{:S(2)}) collective-permute-start(bf16[1,2,128,384]{3,2,1,0:T(8,128)(2,1)} %collective-permute-done.1), channel_id=1, source_target_pairs={{0,15},{1,0},{2,1},{3,2},{4,3},{5,4},{6,5},{7,6},{8,7},{9,8},{10,9... | collective-permute-start | bytes 589832 | tf_op jit(solution)/shard_map/ppermute | solution.py:23
  27.4 7.4 %collective-permute-start.4 = (bf16[1,2,128,384]{3,2,1,0:T(8,128)(2,1)S(1)}, bf16[1,2,128,384]{3,2,1,0:T(8,128)(2,1)S(1)}, u32[]{:S(2)}, u32[]{:S(2)}) collective-permute-start(bf16[1,2,128,384]{3,2,1,0:T(8,128)(2,1)S(1)} %collective-permute-done.2), channel_id=1, source_target_pairs={{0,1},{1,2},{2,3},{3,4},{4,5},{5,6},{6,7},{7,8},{8,9},{9,10},{10,1... | collective-permute-start | bytes 589832 | tf_op jit(solution)/shard_map/ppermute | solution.py:18
  29.9 5.6 %collective-permute-start.5 = (bf16[1,2,128,384]{3,2,1,0:T(8,128)(2,1)S(1)}, bf16[1,2,128,384]{3,2,1,0:T(8,128)(2,1)S(1)}, u32[]{:S(2)}, u32[]{:S(2)}) collective-permute-start(bf16[1,2,128,384]{3,2,1,0:T(8,128)(2,1)S(1)} %collective-permute-done.3), channel_id=1, source_target_pairs={{0,15},{1,0},{2,1},{3,2},{4,3},{5,4},{6,5},{7,6},{8,7},{9,8},{10,9... | collective-permute-start | bytes 589832 | tf_op jit(solution)/shard_map/ppermute | solution.py:23
  34.8 8.6 %collective-permute-start.6 = (bf16[1,2,128,384]{3,2,1,0:T(8,128)(2,1)S(1)}, bf16[1,2,128,384]{3,2,1,0:T(8,128)(2,1)S(1)}, u32[]{:S(2)}, u32[]{:S(2)}) collective-permute-start(bf16[1,2,128,384]{3,2,1,0:T(8,128)(2,1)S(1)} %collective-permute-done.4), channel_id=1, source_target_pairs={{0,1},{1,2},{2,3},{3,4},{4,5},{5,6},{6,7},{7,8},{8,9},{9,10},{10,1... | collective-permute-start | bytes 589832 | tf_op jit(solution)/shard_map/ppermute | solution.py:18
  35.5 8.9 %collective-permute-start.7 = (bf16[1,2,128,384]{3,2,1,0:T(8,128)(2,1)S(1)}, bf16[1,2,128,384]{3,2,1,0:T(8,128)(2,1)S(1)}, u32[]{:S(2)}, u32[]{:S(2)}) collective-permute-start(bf16[1,2,128,384]{3,2,1,0:T(8,128)(2,1)S(1)} %collective-permute-done.5), channel_id=1, source_target_pairs={{0,15},{1,0},{2,1},{3,2},{4,3},{5,4},{6,5},{7,6},{8,7},{9,8},{10,9... | collective-permute-start | bytes 589832 | tf_op jit(solution)/shard_map/ppermute | solution.py:23
  43.4 11.2 %collective-permute-start.8 = (bf16[1,2,128,384]{3,2,1,0:T(8,128)(2,1)S(1)}, bf16[1,2,128,384]{3,2,1,0:T(8,128)(2,1)S(1)}, u32[]{:S(2)}, u32[]{:S(2)}) collective-permute-start(bf16[1,2,128,384]{3,2,1,0:T(8,128)(2,1)S(1)} %collective-permute-done.6), channel_id=1, source_target_pairs={{0,1},{1,2},{2,3},{3,4},{4,5},{5,6},{6,7},{7,8},{8,9},{9,10},{10,1... | collective-permute-start | bytes 589832 | tf_op jit(solution)/shard_map/ppermute | solution.py:18
  44.4 11.3 %collective-permute-start.9 = (bf16[1,2,128,384]{3,2,1,0:T(8,128)(2,1)S(1)}, bf16[1,2,128,384]{3,2,1,0:T(8,128)(2,1)S(1)}, u32[]{:S(2)}, u32[]{:S(2)}) collective-permute-start(bf16[1,2,128,384]{3,2,1,0:T(8,128)(2,1)S(1)} %collective-permute-done.7), channel_id=1, source_target_pairs={{0,15},{1,0},{2,1},{3,2},{4,3},{5,4},{6,5},{7,6},{8,7},{9,8},{10,9... | collective-permute-start | bytes 589832 | tf_op jit(solution)/shard_map/ppermute | solution.py:23
  54.7 8.6 %collective-permute-start.10 = (bf16[1,2,128,384]{3,2,1,0:T(8,128)(2,1)S(1)}, bf16[1,2,128,384]{3,2,1,0:T(8,128)(2,1)S(1)}, u32[]{:S(2)}, u32[]{:S(2)}) collective-permute-start(bf16[1,2,128,384]{3,2,1,0:T(8,128)(2,1)S(1)} %collective-permute-done.8), channel_id=1, source_target_pairs={{0,1},{1,2},{2,3},{3,4},{4,5},{5,6},{6,7},{7,8},{8,9},{9,10},{10,1... | collective-permute-start | bytes 589832 | tf_op jit(solution)/shard_map/ppermute | solution.py:18
  55.7 8.2 %collective-permute-start.11 = (bf16[1,2,128,384]{3,2,1,0:T(8,128)(2,1)S(1)}, bf16[1,2,128,384]{3,2,1,0:T(8,128)(2,1)S(1)}, u32[]{:S(2)}, u32[]{:S(2)}) collective-permute-start(bf16[1,2,128,384]{3,2,1,0:T(8,128)(2,1)S(1)} %collective-permute-done.9), channel_id=1, source_target_pairs={{0,15},{1,0},{2,1},{3,2},{4,3},{5,4},{6,5},{7,6},{8,7},{9,8},{10,9... | collective-permute-start | bytes 589832 | tf_op jit(solution)/shard_map/ppermute | solution.py:23
  63.3 7.9 %collective-permute-start.12 = (bf16[1,2,128,384]{3,2,1,0:T(8,128)(2,1)S(1)}, bf16[1,2,128,384]{3,2,1,0:T(8,128)(2,1)S(1)}, u32[]{:S(2)}, u32[]{:S(2)}) collective-permute-start(bf16[1,2,128,384]{3,2,1,0:T(8,128)(2,1)S(1)} %collective-permute-done.10), channel_id=1, source_target_pairs={{0,1},{1,2},{2,3},{3,4},{4,5},{5,6},{6,7},{7,8},{8,9},{9,10},{10,1... | collective-permute-start | bytes 589832 | tf_op jit(solution)/shard_map/ppermute | solution.py:18
  63.8 7.9 %collective-permute-start.13 = (bf16[1,2,128,384]{3,2,1,0:T(8,128)(2,1)S(1)}, bf16[1,2,128,384]{3,2,1,0:T(8,128)(2,1)S(1)}, u32[]{:S(2)}, u32[]{:S(2)}) collective-permute-start(bf16[1,2,128,384]{3,2,1,0:T(8,128)(2,1)S(1)} %collective-permute-done.11), channel_id=1, source_target_pairs={{0,15},{1,0},{2,1},{3,2},{4,3},{5,4},{6,5},{7,6},{8,7},{9,8},{10,9... | collective-permute-start | bytes 589832 | tf_op jit(solution)/shard_map/ppermute | solution.py:23
  71.2 7.8 %collective-permute-start.14 = (bf16[1,2,128,384]{3,2,1,0:T(8,128)(2,1)S(1)}, bf16[1,2,128,384]{3,2,1,0:T(8,128)(2,1)S(1)}, u32[]{:S(2)}, u32[]{:S(2)}) collective-permute-start(bf16[1,2,128,384]{3,2,1,0:T(8,128)(2,1)S(1)} %collective-permute-done.12), channel_id=1, source_target_pairs={{0,1},{1,2},{2,3},{3,4},{4,5},{5,6},{6,7},{7,8},{8,9},{9,10},{10,1... | collective-permute-start | bytes 589832 | tf_op jit(solution)/shard_map/ppermute | solution.py:18
  79.0 6.6 %copy-start.3 = (bf16[1,32,128,384]{3,2,1,0:T(8,128)(2,1)}, bf16[1,32,128,384]{3,2,1,0:T(8,128)(2,1)S(1)}, u32[]{:S(2)}) copy-start(bf16[1,32,128,384]{3,2,1,0:T(8,128)(2,1)S(1)} %constant_dynamic-update-slice_fusion) | copy-start | bytes 9437188
  93.7 14.2 %collective-permute-start.15 = (bf16[3,1,128,384]{3,2,1,0:T(8,128)(2,1)S(1)}, bf16[3,1,128,384]{3,2,1,0:T(8,128)(2,1)S(1)}, u32[]{:S(2)}, u32[]{:S(2)}) collective-permute-start(bf16[3,1,128,384]{3,2,1,0:T(8,128)(2,1)S(1)} %get-tuple-element.33), channel_id=1, source_target_pairs={{0,1},{1,2},{2,3},{3,4},{4,5},{5,6},{6,7},{7,8},{8,9},{9,10},{10,1... | collective-permute-start | bytes 884744 | tf_op jit(solution)/shard_map/ppermute | solution.py:37
  95.7 12.3 %collective-permute-start.16 = (bf16[3,1,128,384]{3,2,1,0:T(8,128)(2,1)S(1)}, bf16[3,1,128,384]{3,2,1,0:T(8,128)(2,1)S(1)}, u32[]{:S(2)}, u32[]{:S(2)}) collective-permute-start(bf16[3,1,128,384]{3,2,1,0:T(8,128)(2,1)S(1)} %get-tuple-element.34), channel_id=1, source_target_pairs={{1,0},{2,1},{3,2},{4,3},{5,4},{6,5},{7,6},{8,7},{9,8},{10,9},{11,1... | collective-permute-start | bytes 884744 | tf_op jit(solution)/shard_map/ppermute | solution.py:38
  113.4 5.7 %copy-start.8 = (bf16[3,3,384,192]{2,3,1,0:T(8,128)(2,1)S(1)}, bf16[3,3,384,192]{2,3,1,0:T(8,128)(2,1)}, u32[]{:S(2)}) copy-start(bf16[3,3,384,192]{2,3,1,0:T(8,128)(2,1)} %param.19) | copy-start | bytes 3981316
  114.6 8.4 %collective-permute-start.17 = (bf16[1,1,128,384]{3,2,1,0:T(8,128)(2,1)S(1)}, bf16[1,1,128,384]{3,2,1,0:T(8,128)(2,1)S(1)}, u32[]{:S(2)}, u32[]{:S(2)}) collective-permute-start(bf16[1,1,128,384]{3,2,1,0:T(8,128)(2,1)S(1)} %get-tuple-element.35), channel_id=1, source_target_pairs={{0,1},{1,2},{2,3},{3,4},{4,5},{5,6},{6,7},{7,8},{8,9},{9,10},{10,1... | collective-permute-start | bytes 294920 | tf_op jit(solution)/shard_map/ppermute | solution.py:37
  116.5 6.5 %collective-permute-start.18 = (bf16[1,1,128,384]{3,2,1,0:T(8,128)(2,1)S(1)}, bf16[1,1,128,384]{3,2,1,0:T(8,128)(2,1)S(1)}, u32[]{:S(2)}, u32[]{:S(2)}) collective-permute-start(bf16[1,1,128,384]{3,2,1,0:T(8,128)(2,1)S(1)} %get-tuple-element.36), channel_id=1, source_target_pairs={{1,0},{2,1},{3,2},{4,3},{5,4},{6,5},{7,6},{8,7},{9,8},{10,9},{11,1... | collective-permute-start | bytes 294920 | tf_op jit(solution)/shard_map/ppermute | solution.py:38
  (8 other events, 21.5 us)
Sparse Core Ops, SparseCore 0:
  10.8 56.4 all-gather.1
